TPU v7x, 256 devices: a whole 4x4x8 slice. The times are simulated.
256 devices in a mesh: tm: 2 (over core), tile: 128 (over x, z, y).
Axes of the slice: x: 4, y: 4, z: 8, core: 2. Of those that a mesh axis runs over, the one named last changes fastest.
Arguments:
- features: bfloat16 [4, 128, 128, 384], P('tm', 'tile'), may hold values from -48 to 48
- query_weight: bfloat16 [384, 384], replicated, may hold values from -1 to 1
- key_weight: bfloat16 [384, 384], replicated, may hold values from -12 to 12
- value_weight: bfloat16 [384, 384], replicated, may hold values from -0.3125 to 0.3125
- out_weight: bfloat16 [384, 384], replicated, may hold values from -1.25 to 1.25
- conv_weight: bfloat16 [3, 3, 3, 384, 384], replicated, may hold values from -0.0625 to 0.0625
Outputs:
- decoded: bfloat16 [4, 128, 128, 384], P('tm', 'tile')
All inputs are finite; a program needn't handle non-finite values.
Results may differ from a plain program's by a relative error of at most 0.019.
Values may be sent and summed in bfloat16 or wider, within the bound.
No kernel may reach another device: no remote copies, remote signals or barrier semaphores. Data moves between devices by JAX's collectives and lax.ppermute only.
A program may use at most 128 MiB of HBM per device.

v0:
```python
import math

import jax
import jax.numpy as jnp
from jax import lax
from jax.sharding import PartitionSpec as P


def partner_2(shard, axis, stride):
    return lax.ppermute(shard, axis, [(i, i ^ 1 << stride) for i in range(lax.axis_size(axis))])


def for_sending(shard):

    def short(part):
        return part.astype(jnp.bfloat16) if part.dtype == jnp.float32 else part

    return jax.tree.map(short, shard)


def from_behind(block, axis, distance):
    devices = range(lax.axis_size(axis))
    route = [(i - distance, i) for i in devices if i - distance in devices]
    return lax.ppermute(block, axis, route)


def padded_2(cells, sides, width):
    for axis, dim in sides:
        count = lax.axis_size(axis)
        ends = count - 1
        head = lax.slice_in_dim(cells, 0, width, axis=dim)
        tail = lax.slice_in_dim(cells, cells.shape[dim] - width, cells.shape[dim], axis=dim)
        cells = jnp.concatenate(
            [
                lax.ppermute(tail, axis, [(i, (i + 1) % count) for i in range(ends)]),
                cells,
                lax.ppermute(head, axis, [((i + 1) % count, i) for i in range(ends)]),
            ],
            axis=dim,
        )
    return cells


def rms_rows(values):
    return values * lax.rsqrt(jnp.mean(values * values, axis=-1, keepdims=True) + 1e-06)


def project(flat_rows, weight):
    return jnp.dot(flat_rows, weight, preferred_element_type=jnp.float32).astype(jnp.bfloat16)


def ordered_join(mine, other, upper):
    low_first = jnp.concatenate([mine, other], axis=0)
    high_first = jnp.concatenate([other, mine], axis=0)
    return jnp.where(upper == 0, low_first, high_first)


def combine_partials(first, second):
    high_a, total_a, summed_a = first
    high_b, total_b, summed_b = second
    fresh = jnp.maximum(high_a, high_b)
    weight_a = jnp.exp(high_a - fresh)
    weight_b = jnp.exp(high_b - fresh)
    total = total_a * weight_a + total_b * weight_b
    summed = summed_a * weight_a[..., None] + summed_b * weight_b[..., None]
    return (fresh, total, summed)


def per_device(features, query_weight, key_weight, value_weight, out_weight, conv_weight):
    frames, rows, cols, width = features.shape
    count = rows * cols
    widened = features.astype(jnp.float32)
    normed = rms_rows(widened).astype(jnp.bfloat16)
    flat = normed.reshape(frames * count, width)
    scale = 1.0 / math.sqrt(width)
    all_bits = lax.axis_size("tile").bit_length() - 1
    query_bits = all_bits // 2
    key_bits = all_bits - query_bits
    position = lax.axis_index("tile")
    query_stack = project(flat, query_weight).reshape(1, frames, count, width)
    for level in range(key_bits, all_bits):
        upper = position // (1 << level) % 2
        partner = partner_2(query_stack, "tile", level)
        query_stack = ordered_join(query_stack, partner, upper)
    key_rows = project(flat, key_weight).reshape(frames, count, width)
    value_rows = project(flat, value_weight).reshape(frames, count, width)
    for level in range(key_bits):
        other_keys, other_values = partner_2((key_rows, value_rows), "tile", level)
        key_rows = jnp.concatenate([key_rows, other_keys], axis=1)
        value_rows = jnp.concatenate([value_rows, other_values], axis=1)
    scores = (
        jnp.einsum("mfqd,fkd->mfqk", query_stack, key_rows, preferred_element_type=jnp.float32)
        * scale
    )
    highest = jnp.max(scores, axis=-1)
    expo = jnp.exp(scores - highest[..., None])
    total = jnp.sum(expo, axis=-1)
    probs = expo.astype(jnp.bfloat16)
    summed = jnp.einsum("mfqk,fkd->mfqd", probs, value_rows, preferred_element_type=jnp.float32)
    state = (highest, total, summed)
    for level in reversed(range(key_bits, all_bits)):
        upper = position // (1 << level) % 2
        half = state[0].shape[0] // 2
        kept = tuple((jnp.where(upper == 0, part[:half], part[half:]) for part in state))
        sent = tuple((jnp.where(upper == 0, part[half:], part[:half]) for part in state))
        came = partner_2(
            (for_sending(sent[0]), for_sending(sent[1]), for_sending(sent[2])), "tile", level
        )
        state = combine_partials(kept, came)
    highest, total, summed = (state[0][0], state[1][0], state[2][0])
    attended = (summed / total[:, :, None]).astype(jnp.bfloat16)
    projected = jnp.dot(attended.reshape(-1, width), out_weight, preferred_element_type=jnp.float32)
    mixed = (widened + projected.reshape(features.shape)).astype(jnp.bfloat16)
    mixed_wide = mixed.astype(jnp.float32)
    activated = jax.nn.silu(rms_rows(mixed_wide)).astype(jnp.bfloat16)
    earlier = from_behind(activated, "tm", 1)
    stacked = jnp.concatenate([earlier, activated], axis=0)
    padded = padded_2(stacked, (("tile", 1),), 1)
    padded = jnp.pad(padded, ((0, 0), (0, 0), (1, 1), (0, 0)))
    patches = []
    for tap_time in range(3):
        for tap_row in range(3):
            for tap_col in range(3):
                patches.append(
                    padded[
                        tap_time : tap_time + frames,
                        tap_row : tap_row + rows,
                        tap_col : tap_col + cols,
                    ]
                )
    columns = jnp.concatenate(patches, axis=-1).reshape(frames * count, 27 * width)
    conv = jnp.dot(
        columns, conv_weight.reshape(27 * width, width), preferred_element_type=jnp.float32
    )
    return (mixed_wide + conv.reshape(features.shape)).astype(jnp.bfloat16)


def solution(mesh):
    in_specs = (P("tm", "tile", None, None), P(), P(), P(), P(), P())
    out_specs = P("tm", "tile", None, None)
    return jax.shard_map(
        per_device, mesh=mesh, in_specs=in_specs, out_specs=out_specs, check_vma=False
    )
```

profile of v0, /device:TPU:2, one launch (start us, length us, event | category | flops | bytes accessed | tf_op | source)
XLA Modules:
  0.0 274.5 jit_solution(14219000844744878070)
XLA Ops:
  0.0 1.1 fusion.42
  1.1 1.0 fusion.43
  2.2 1.2 convolution_convert_fusion.1
  3.4 1.7 collective-permute-start.4
  5.1 5.1 %collective-permute-done.4 = bf16[2,128,384]{2,1,0:T(8,128)(2,1)S(1)} collective-permute-done((bf16[2,128,384]{2,1,0:T(8,128)(2,1)S(1)}, bf16[2,128,384]{2,1,0:T(8,128)(2,1)S(1)}, u32[]{:S(2)}, u32[]{:S(2)}) %collective-permute-start.4) | collective-permute-done | bytes 196640 | tf_op jit(solution)/shard_map/ppermute | solution.py:10
  10.2 3.3 %collective-permute-start.5 = (bf16[2,256,384]{2,1,0:T(8,128)(2,1)S(1)}, bf16[2,256,384]{2,1,0:T(8,128)(2,1)S(1)}, u32[]{:S(2)}, u32[]{:S(2)}) collective-permute-start(bf16[2,256,384]{2,1,0:T(8,128)(2,1)S(1)} %pad_maximum_fusion.6), channel_id=1, source_target_pairs={{0,2},{1,3},{2,0},{3,1},{4,6},{5,7},{6,4},{7,5},{8,10},{9,11},{10,... | collective-permute-start | bytes 1179656 | tf_op jit(solution)/shard_map/ppermute | solution.py:10
  13.4 8.3 %collective-permute-done.5 = bf16[2,256,384]{2,1,0:T(8,128)(2,1)S(1)} collective-permute-done((bf16[2,256,384]{2,1,0:T(8,128)(2,1)S(1)}, bf16[2,256,384]{2,1,0:T(8,128)(2,1)S(1)}, u32[]{:S(2)}, u32[]{:S(2)}) %collective-permute-start.5) | collective-permute-done | bytes 393248 | tf_op jit(solution)/shard_map/ppermute | solution.py:10
  21.8 1.0 pad_maximum_fusion.3
  22.7 1.9 collective-permute-start.6
  24.6 0.3 convolution_convert_fusion.2
  24.9 0.2 copy.12
  25.1 1.7 collective-permute-start
  26.8 4.1 %collective-permute-done = bf16[2,128,384]{1,2,0:T(8,128)(2,1)S(1)} collective-permute-done((bf16[2,128,384]{1,2,0:T(8,128)(2,1)S(1)}, bf16[2,128,384]{1,2,0:T(8,128)(2,1)S(1)}, u32[]{:S(2)}, u32[]{:S(2)}) %collective-permute-start) | collective-permute-done | bytes 196640 | tf_op jit(solution)/shard_map/ppermute | solution.py:10
  30.9 3.3 %collective-permute-start.1 = (bf16[2,256,384]{1,2,0:T(8,128)(2,1)S(1)}, bf16[2,256,384]{1,2,0:T(8,128)(2,1)S(1)}, u32[]{:S(2)}, u32[]{:S(2)}) collective-permute-start(bf16[2,256,384]{1,2,0:T(8,128)(2,1)S(1)} %pad_maximum_fusion.5), channel_id=1, source_target_pairs={{0,2},{1,3},{2,0},{3,1},{4,6},{5,7},{6,4},{7,5},{8,10},{9,11},{10,... | collective-permute-start | bytes 1179656 | tf_op jit(solution)/shard_map/ppermute | solution.py:10
  34.2 1.2 convolution_convert_fusion
  35.4 6.4 %collective-permute-start.8 = (bf16[1,2,128,384]{3,2,0,1:T(8,128)(2,1)S(1)}, bf16[1,2,128,384]{3,2,0,1:T(8,128)(2,1)S(1)}, u32[]{:S(2)}, u32[]{:S(2)}) collective-permute-start(bf16[1,2,128,384]{3,2,0,1:T(8,128)(2,1)S(1)} %bitcast.103), channel_id=1, source_target_pairs={{0,16},{1,17},{2,18},{3,19},{4,20},{5,21},{6,22},{7,23},{8,24},{9,... | collective-permute-start | bytes 589832 | tf_op jit(solution)/shard_map/ppermute | solution.py:10
  41.8 1.3 pad_maximum_fusion.1
  43.2 6.9 %collective-permute-start.7 = (bf16[2,1024,384]{2,1,0:T(8,128)(2,1)}, bf16[2,1024,384]{2,1,0:T(8,128)(2,1)}, u32[]{:S(2)}, u32[]{:S(2)}) collective-permute-start(bf16[2,1024,384]{2,1,0:T(8,128)(2,1)} %pad_maximum_fusion.1), channel_id=1, source_target_pairs={{0,8},{1,9},{2,10},{3,11},{4,12},{5,13},{6,14},{7,15},{8,0},{9,1},... | collective-permute-start | bytes 4718600 | tf_op jit(solution)/shard_map/ppermute | solution.py:10
  50.1 7.9 %collective-permute-done.8 = bf16[1,2,128,384]{3,2,0,1:T(8,128)(2,1)S(1)} collective-permute-done((bf16[1,2,128,384]{3,2,0,1:T(8,128)(2,1)S(1)}, bf16[1,2,128,384]{3,2,0,1:T(8,128)(2,1)S(1)}, u32[]{:S(2)}, u32[]{:S(2)}) %collective-permute-start.8) | collective-permute-done | bytes 196640 | tf_op jit(solution)/shard_map/ppermute | solution.py:10
  58.0 0.8 maximum_select_fusion.3
  58.8 0.5 collective-permute-start.9
  59.3 1.0 pad_maximum_fusion.2
  60.3 0.7 constant_dynamic-update-slice_fusion.9
  61.0 0.7 constant_dynamic-update-slice_fusion.8
  61.8 8.6 %collective-permute-done.9 = bf16[2,2,128,384]{3,2,0,1:T(8,128)(2,1)} collective-permute-done((bf16[2,2,128,384]{3,2,0,1:T(8,128)(2,1)}, bf16[2,2,128,384]{3,2,0,1:T(8,128)(2,1)}, u32[]{:S(2)}, u32[]{:S(2)}) %collective-permute-start.9) | collective-permute-done | bytes 393248 | tf_op jit(solution)/shard_map/ppermute | solution.py:10
  70.4 1.5 maximum_select_fusion.2
  71.9 2.9 %collective-permute-start.10 = (bf16[4,2,128,384]{3,2,0,1:T(8,128)(2,1)S(1)}, bf16[4,2,128,384]{3,2,0,1:T(8,128)(2,1)S(1)}, u32[]{:S(2)}, u32[]{:S(2)}) collective-permute-start(bf16[4,2,128,384]{3,2,0,1:T(8,128)(2,1)S(1)} %maximum_select_fusion.2), channel_id=1, source_target_pairs={{0,64},{1,65},{2,66},{3,67},{4,68},{5,69},{6,70},{7,71},{8,72},{9,... | collective-permute-start | bytes 2359304 | tf_op jit(solution)/shard_map/ppermute | solution.py:10
  74.8 0.8 constant_dynamic-update-slice_fusion.7
  75.6 23.8 %collective-permute-done.2 = bf16[2,512,384]{1,2,0:T(8,128)(2,1)S(1)} collective-permute-done((bf16[2,512,384]{1,2,0:T(8,128)(2,1)}, bf16[2,512,384]{1,2,0:T(8,128)(2,1)S(1)}, u32[]{:S(2)}, u32[]{:S(2)}) %collective-permute-start.2) | collective-permute-done | bytes 786464 | tf_op jit(solution)/shard_map/ppermute | solution.py:10
  99.4 0.2 pad_maximum_fusion
  99.7 4.7 %collective-permute-start.3 = (bf16[2,1024,384]{1,2,0:T(8,128)(2,1)S(1)}, bf16[2,1024,384]{1,2,0:T(8,128)(2,1)S(1)}, u32[]{:S(2)}, u32[]{:S(2)}) collective-permute-start(bf16[2,1024,384]{1,2,0:T(8,128)(2,1)S(1)} %pad_maximum_fusion), channel_id=1, source_target_pairs={{0,8},{1,9},{2,10},{3,11},{4,12},{5,13},{6,14},{7,15},{8,0},{9,1},... | collective-permute-start | bytes 4718600 | tf_op jit(solution)/shard_map/ppermute | solution.py:10
  104.6 48.4 %collective-permute-done.7 = bf16[2,1024,384]{2,1,0:T(8,128)(2,1)} collective-permute-done((bf16[2,1024,384]{2,1,0:T(8,128)(2,1)}, bf16[2,1024,384]{2,1,0:T(8,128)(2,1)}, u32[]{:S(2)}, u32[]{:S(2)}) %collective-permute-start.7) | collective-permute-done | bytes 1572896 | tf_op jit(solution)/shard_map/ppermute | solution.py:10
  153.0 1.7 constant_dynamic-update-slice_fusion.5
  154.8 8.1 %bitcast_reduce_fusion = (f32[8,2,128]{2,0,1:T(8,128)S(1)}, f32[2,2048,8,128]{3,1,2,0:T(8,128)}) fusion(bf16[4,2,128,384]{3,2,0,1:T(8,128)(2,1)S(1)} %collective-permute-done.10, bf16[4,2,128,384]{3,2,0,1:T(8,128)(2,1)S(1)} %maximum_select_fusion.2, pred[]{:T(512)S(6)} %eq.15, bf16[2,2048,384]{2,1,0:T(8,128)(2,1)S(1)} %constant_dynamic-update-slice_fusion.5), kind=kOutput, calls=%fused_computation.1 | convolution fusion | flops 3236689920 | bytes 21504000 | tf_op jit(solution)/shard_map/mfqd,fkd->mfqk/dot_general | solution.py:92
  162.9 8.7 %fusion.1 = f32[8,2,128]{2,0,1:T(8,128)S(1)} fusion(f32[2,2048,8,128]{3,1,2,0:T(8,128)} %get-tuple-element.17, f32[8,2,128]{2,0,1:T(8,128)S(1)} %get-tuple-element.16), kind=kLoop, calls=%fused_computation.3 | loop fusion | flops 12580864 | bytes 16793600 | tf_op jit(solution)/shard_map/reduce_sum | solution.py:97
  171.6 14.0 %collective-permute-done.3 = bf16[2,1024,384]{1,2,0:T(8,128)(2,1)S(1)} collective-permute-done((bf16[2,1024,384]{1,2,0:T(8,128)(2,1)S(1)}, bf16[2,1024,384]{1,2,0:T(8,128)(2,1)S(1)}, u32[]{:S(2)}, u32[]{:S(2)}) %collective-permute-start.3) | collective-permute-done | bytes 1572896 | tf_op jit(solution)/shard_map/ppermute | solution.py:10
  185.8 7.7 %fusion.13 = f32[8,2,128,384]{2,3,0,1:T(8,128)S(1)} fusion(f32[2,2048,8,128]{3,1,2,0:T(8,128)} %get-tuple-element.17, f32[8,2,128]{2,0,1:T(8,128)S(1)} %get-tuple-element.16, bf16[2,2048,384]{1,2,0:T(8,128)(2,1)S(1)} %constant_dynamic-update-slice_fusion), kind=kOutput, calls=%fused_computation.16 | convolution fusion | flops 3233808384 | bytes 23076864 | tf_op jit(solution)/shard_map/mfqk,fkd->mfqd/dot_general | solution.py:99
  193.5 2.2 collective-permute-start.17
  195.7 1.4 collective-permute-start.11
  197.3 2.2 collective-permute-start.12
  199.5 1.3 collective-permute-done.11
  200.9 1.5 collective-permute-start.18
  202.4 0.6 collective-permute-start.13
  203.0 13.9 %collective-permute-done.18 = bf16[2,2,128]{2,0,1:T(2,128)(2,1)S(1)} collective-permute-done((bf16[2,2,128]{2,0,1:T(2,128)(2,1)S(1)}, bf16[2,2,128]{2,0,1:T(2,128)(2,1)S(1)}, u32[]{:S(2)}, u32[]{:S(2)}) %collective-permute-start.18) | collective-permute-done | bytes 1056 | tf_op jit(solution)/shard_map/ppermute | solution.py:10
  217.0 4.1 %collective-permute-start.19 = (bf16[1,2,128]{2,0,1:T(2,128)(2,1)S(1)}, bf16[1,2,128]{2,0,1:T(2,128)(2,1)S(1)}, u32[]{:S(2)}, u32[]{:S(2)}) collective-permute-start(bf16[1,2,128]{2,0,1:T(2,128)(2,1)S(1)} %fusion.60), channel_id=1, source_target_pairs={{0,16},{1,17},{2,18},{3,19},{4,20},{5,21},{6,22},{7,23},{8,24},{9,... | collective-permute-start | bytes 1544 | tf_op jit(solution)/shard_map/ppermute | solution.py:10
  221.1 0.3 multiply_add_fusion
  221.5 0.7 collective-permute-start.14
  222.2 2.3 collective-permute-start.15
  224.5 4.9 %collective-permute-done.14 = bf16[2,2,128,384]{2,3,0,1:T(8,128)(2,1)S(1)} collective-permute-done((bf16[2,2,128,384]{2,3,0,1:T(8,128)(2,1)S(1)}, bf16[2,2,128,384]{2,3,0,1:T(8,128)(2,1)S(1)}, u32[]{:S(2)}, u32[]{:S(2)}) %collective-permute-start.14) | collective-permute-done | bytes 393248 | tf_op jit(solution)/shard_map/ppermute | solution.py:10
  229.4 0.2 multiply_add_fusion.1
  229.6 2.7 collective-permute-start.16
  232.2 8.2 %collective-permute-done.16 = bf16[1,2,128,384]{2,3,0,1:T(8,128)(2,1)S(1)} collective-permute-done((bf16[1,2,128,384]{2,3,0,1:T(8,128)(2,1)S(1)}, bf16[1,2,128,384]{2,3,0,1:T(8,128)(2,1)S(1)}, u32[]{:S(2)}, u32[]{:S(2)}) %collective-permute-start.16) | collective-permute-done | bytes 196640 | tf_op jit(solution)/shard_map/ppermute | solution.py:10
  240.5 0.4 multiply_reduce_fusion
  240.9 0.2 multiply_convert_fusion
  241.1 1.4 collective-permute-start.20
  242.5 1.0 collective-permute-done.20
  243.6 7.3 %collective-permute-start.22 = (bf16[4,1,128,384]{3,2,0,1:T(8,128)(2,1)S(1)}, bf16[4,1,128,384]{3,2,0,1:T(8,128)(2,1)S(1)}, u32[]{:S(2)}, u32[]{:S(2)}) collective-permute-start(bf16[4,1,128,384]{3,2,0,1:T(8,128)(2,1)S(1)} %pad_maximum_fusion.4), channel_id=1, source_target_pairs={{1,0},{2,1},{3,2},{4,3},{5,4},{6,5},{7,6},{8,7},{9,8},{10,9},{11,1... | collective-permute-start | bytes 1179656 | tf_op jit(solution)/shard_map/ppermute | solution.py:37
  251.0 1.9 collective-permute-start.21
  252.9 7.0 %collective-permute-done.22 = bf16[4,1,128,384]{3,2,0,1:T(8,128)(2,1)S(1)} collective-permute-done((bf16[4,1,128,384]{3,2,0,1:T(8,128)(2,1)S(1)}, bf16[4,1,128,384]{3,2,0,1:T(8,128)(2,1)S(1)}, u32[]{:S(2)}, u32[]{:S(2)}) %collective-permute-start.22) | collective-permute-done | bytes 393248 | tf_op jit(solution)/shard_map/ppermute | solution.py:37
  259.9 8.3 %collective-permute-done.21 = bf16[4,1,128,384]{3,2,0,1:T(8,128)(2,1)S(1)} collective-permute-done((bf16[4,1,128,384]{3,2,0,1:T(8,128)(2,1)S(1)}, bf16[4,1,128,384]{3,2,0,1:T(8,128)(2,1)S(1)}, u32[]{:S(2)}, u32[]{:S(2)}) %collective-permute-start.21) | collective-permute-done | bytes 393248 | tf_op jit(solution)/shard_map/ppermute | solution.py:35
  268.2 0.3 select_maximum_fusion
  269.6 0.2 constant_dynamic-update-slice_fusion.10
  270.1 0.8 slice-done.1
  270.9 3.6 %fusion.39 = bf16[2,1,128,384]{3,2,1,0:T(8,128)(2,1)} fusion(f32[2,1,128,384]{3,2,0,1:T(8,128)S(1)} %get-tuple-element.19, bf16[10368,384,1]{1,0,2:T(8,128)(2,1)S(1)} %bitcast.110, bf16[2,1,128,10368]{3,2,0,1:T(8,128)(2,1)S(1)} %slice_dynamic-update-slice_fusion), kind=kOutput, calls=%fused_computation.43 | convolution fusion | flops 2038628352 | bytes 13860864 | tf_op jit(solution)/shard_map/dot_general | solution.py:132
  (75 shorter events, 2.3 us)
Async XLA Ops:
  0.0 240.4 %copy-start = (bf16[384,384]{1,0:T(8,128)(2,1)S(1)}, bf16[384,384]{1,0:T(8,128)(2,1)}, u32[]{:S(2)}) copy-start(bf16[384,384]{1,0:T(8,128)(2,1)} %param.10) | copy-start | bytes 884740
  0.0 24.6 %copy-start.2 = (bf16[384,384]{1,0:T(8,128)(2,1)S(1)}, bf16[384,384]{1,0:T(8,128)(2,1)}, u32[]{:S(2)}) copy-start(bf16[384,384]{1,0:T(8,128)(2,1)} %param.9) | copy-start | bytes 884740
  3.4 6.7 %collective-permute-start.4 = (bf16[2,128,384]{2,1,0:T(8,128)(2,1)S(1)}, bf16[2,128,384]{2,1,0:T(8,128)(2,1)S(1)}, u32[]{:S(2)}, u32[]{:S(2)}) collective-permute-start(bf16[2,128,384]{2,1,0:T(8,128)(2,1)S(1)} %bitcast.94), channel_id=1, source_target_pairs={{0,1},{1,0},{2,3},{3,2},{4,5},{5,4},{6,7},{7,6},{8,9},{9,8},{10,11... | collective-permute-start | bytes 589832 | tf_op jit(solution)/shard_map/ppermute | solution.py:10
  10.2 11.6 %collective-permute-start.5 = (bf16[2,256,384]{2,1,0:T(8,128)(2,1)S(1)}, bf16[2,256,384]{2,1,0:T(8,128)(2,1)S(1)}, u32[]{:S(2)}, u32[]{:S(2)}) collective-permute-start(bf16[2,256,384]{2,1,0:T(8,128)(2,1)S(1)} %pad_maximum_fusion.6), channel_id=1, source_target_pairs={{0,2},{1,3},{2,0},{3,1},{4,6},{5,7},{6,4},{7,5},{8,10},{9,11},{10,... | collective-permute-start | bytes 1179656 | tf_op jit(solution)/shard_map/ppermute | solution.py:10
  22.7 19.1 %collective-permute-start.6 = (bf16[2,512,384]{2,1,0:T(8,128)(2,1)}, bf16[2,512,384]{2,1,0:T(8,128)(2,1)S(1)}, u32[]{:S(2)}, u32[]{:S(2)}) collective-permute-start(bf16[2,512,384]{2,1,0:T(8,128)(2,1)} %pad_maximum_fusion.3), channel_id=1, source_target_pairs={{0,4},{1,5},{2,6},{3,7},{4,0},{5,1},{6,2},{7,3},{8,12},{9,13},{10,... | collective-permute-start | bytes 2359304 | tf_op jit(solution)/shard_map/ppermute | solution.py:10
  25.1 5.8 %collective-permute-start = (bf16[2,128,384]{1,2,0:T(8,128)(2,1)S(1)}, bf16[2,128,384]{1,2,0:T(8,128)(2,1)S(1)}, u32[]{:S(2)}, u32[]{:S(2)}) collective-permute-start(bf16[2,128,384]{1,2,0:T(8,128)(2,1)S(1)} %copy.12), channel_id=1, source_target_pairs={{0,1},{1,0},{2,3},{3,2},{4,5},{5,4},{6,7},{7,6},{8,9},{9,8},{10,11... | collective-permute-start | bytes 589832 | tf_op jit(solution)/shard_map/ppermute | solution.py:10
  30.9 28.4 %collective-permute-start.1 = (bf16[2,256,384]{1,2,0:T(8,128)(2,1)S(1)}, bf16[2,256,384]{1,2,0:T(8,128)(2,1)S(1)}, u32[]{:S(2)}, u32[]{:S(2)}) collective-permute-start(bf16[2,256,384]{1,2,0:T(8,128)(2,1)S(1)} %pad_maximum_fusion.5), channel_id=1, source_target_pairs={{0,2},{1,3},{2,0},{3,1},{4,6},{5,7},{6,4},{7,5},{8,10},{9,11},{10,... | collective-permute-start | bytes 1179656 | tf_op jit(solution)/shard_map/ppermute | solution.py:10
  35.4 22.5 %collective-permute-start.8 = (bf16[1,2,128,384]{3,2,0,1:T(8,128)(2,1)S(1)}, bf16[1,2,128,384]{3,2,0,1:T(8,128)(2,1)S(1)}, u32[]{:S(2)}, u32[]{:S(2)}) collective-permute-start(bf16[1,2,128,384]{3,2,0,1:T(8,128)(2,1)S(1)} %bitcast.103), channel_id=1, source_target_pairs={{0,16},{1,17},{2,18},{3,19},{4,20},{5,21},{6,22},{7,23},{8,24},{9,... | collective-permute-start | bytes 589832 | tf_op jit(solution)/shard_map/ppermute | solution.py:10
  43.2 109.9 %collective-permute-start.7 = (bf16[2,1024,384]{2,1,0:T(8,128)(2,1)}, bf16[2,1024,384]{2,1,0:T(8,128)(2,1)}, u32[]{:S(2)}, u32[]{:S(2)}) collective-permute-start(bf16[2,1024,384]{2,1,0:T(8,128)(2,1)} %pad_maximum_fusion.1), channel_id=1, source_target_pairs={{0,8},{1,9},{2,10},{3,11},{4,12},{5,13},{6,14},{7,15},{8,0},{9,1},... | collective-permute-start | bytes 4718600 | tf_op jit(solution)/shard_map/ppermute | solution.py:10
  58.8 11.6 %collective-permute-start.9 = (bf16[2,2,128,384]{3,2,0,1:T(8,128)(2,1)}, bf16[2,2,128,384]{3,2,0,1:T(8,128)(2,1)}, u32[]{:S(2)}, u32[]{:S(2)}) collective-permute-start(bf16[2,2,128,384]{3,2,0,1:T(8,128)(2,1)} %maximum_select_fusion.3), channel_id=1, source_target_pairs={{0,32},{1,33},{2,34},{3,35},{4,36},{5,37},{6,38},{7,39},{8,40},{9,... | collective-permute-start | bytes 1179656 | tf_op jit(solution)/shard_map/ppermute | solution.py:10
  60.3 39.2 %collective-permute-start.2 = (bf16[2,512,384]{1,2,0:T(8,128)(2,1)}, bf16[2,512,384]{1,2,0:T(8,128)(2,1)S(1)}, u32[]{:S(2)}, u32[]{:S(2)}) collective-permute-start(bf16[2,512,384]{1,2,0:T(8,128)(2,1)} %pad_maximum_fusion.2), channel_id=1, source_target_pairs={{0,4},{1,5},{2,6},{3,7},{4,0},{5,1},{6,2},{7,3},{8,12},{9,13},{10,... | collective-permute-start | bytes 2359304 | tf_op jit(solution)/shard_map/ppermute | solution.py:10
  71.9 82.9 %collective-permute-start.10 = (bf16[4,2,128,384]{3,2,0,1:T(8,128)(2,1)S(1)}, bf16[4,2,128,384]{3,2,0,1:T(8,128)(2,1)S(1)}, u32[]{:S(2)}, u32[]{:S(2)}) collective-permute-start(bf16[4,2,128,384]{3,2,0,1:T(8,128)(2,1)S(1)} %maximum_select_fusion.2), channel_id=1, source_target_pairs={{0,64},{1,65},{2,66},{3,67},{4,68},{5,69},{6,70},{7,71},{8,72},{9,... | collective-permute-start | bytes 2359304 | tf_op jit(solution)/shard_map/ppermute | solution.py:10
  75.6 28.8 %copy-start.3 = (bf16[2,2048,384]{2,1,0:T(8,128)(2,1)S(1)}, bf16[2,2048,384]{2,1,0:T(8,128)(2,1)}, u32[]{:S(2)}) copy-start(bf16[2,2048,384]{2,1,0:T(8,128)(2,1)} %constant_dynamic-update-slice_fusion.7) | copy-start | bytes 9437188
  99.7 86.0 %collective-permute-start.3 = (bf16[2,1024,384]{1,2,0:T(8,128)(2,1)S(1)}, bf16[2,1024,384]{1,2,0:T(8,128)(2,1)S(1)}, u32[]{:S(2)}, u32[]{:S(2)}) collective-permute-start(bf16[2,1024,384]{1,2,0:T(8,128)(2,1)S(1)} %pad_maximum_fusion), channel_id=1, source_target_pairs={{0,8},{1,9},{2,10},{3,11},{4,12},{5,13},{6,14},{7,15},{8,0},{9,1},... | collective-permute-start | bytes 4718600 | tf_op jit(solution)/shard_map/ppermute | solution.py:10
  104.6 50.2 %copy-start.4 = (bf16[2,2048,384]{1,2,0:T(8,128)(2,1)}, bf16[2,2048,384]{1,2,0:T(8,128)(2,1)S(1)}, u32[]{:S(2)}) copy-start(bf16[2,2048,384]{1,2,0:T(8,128)(2,1)S(1)} %constant_dynamic-update-slice_fusion.1) | copy-start | bytes 9437188
  162.9 22.7 %copy-start.5 = (bf16[2,2048,384]{1,2,0:T(8,128)(2,1)S(1)}, bf16[2,2048,384]{1,2,0:T(8,128)(2,1)}, u32[]{:S(2)}) copy-start(bf16[2,2048,384]{1,2,0:T(8,128)(2,1)} %copy-done.4) | copy-start | bytes 9437188
  193.5 6.0 %collective-permute-start.17 = (bf16[4,2,128]{2,0,1:T(4,128)(2,1)S(1)}, bf16[4,2,128]{2,0,1:T(4,128)(2,1)S(1)}, u32[]{:S(2)}, u32[]{:S(2)}) collective-permute-start(bf16[4,2,128]{2,0,1:T(4,128)(2,1)S(1)} %select_convert_fusion.3), channel_id=1, source_target_pairs={{0,64},{1,65},{2,66},{3,67},{4,68},{5,69},{6,70},{7,71},{8,72},{9,... | collective-permute-start | bytes 6152 | tf_op jit(solution)/shard_map/ppermute | solution.py:10
  195.7 5.1 %collective-permute-start.11 = (bf16[4,2,128]{2,0,1:T(4,128)(2,1)S(1)}, bf16[4,2,128]{2,0,1:T(4,128)(2,1)S(1)}, u32[]{:S(2)}, u32[]{:S(2)}) collective-permute-start(bf16[4,2,128]{2,0,1:T(4,128)(2,1)S(1)} %select_convert_fusion.4), channel_id=1, source_target_pairs={{0,64},{1,65},{2,66},{3,67},{4,68},{5,69},{6,70},{7,71},{8,72},{9,... | collective-permute-start | bytes 6152 | tf_op jit(solution)/shard_map/ppermute | solution.py:10
  197.3 23.8 %collective-permute-start.12 = (bf16[4,2,128,384]{2,3,0,1:T(8,128)(2,1)S(1)}, bf16[4,2,128,384]{2,3,0,1:T(8,128)(2,1)S(1)}, u32[]{:S(2)}, u32[]{:S(2)}) collective-permute-start(bf16[4,2,128,384]{2,3,0,1:T(8,128)(2,1)S(1)} %select_convert_fusion), channel_id=1, source_target_pairs={{0,64},{1,65},{2,66},{3,67},{4,68},{5,69},{6,70},{7,71},{8,72},{9,... | collective-permute-start | bytes 2359304 | tf_op jit(solution)/shard_map/ppermute | solution.py:10
  200.9 16.1 %collective-permute-start.18 = (bf16[2,2,128]{2,0,1:T(2,128)(2,1)S(1)}, bf16[2,2,128]{2,0,1:T(2,128)(2,1)S(1)}, u32[]{:S(2)}, u32[]{:S(2)}) collective-permute-start(bf16[2,2,128]{2,0,1:T(2,128)(2,1)S(1)} %select_convert_fusion.5), channel_id=1, source_target_pairs={{0,32},{1,33},{2,34},{3,35},{4,36},{5,37},{6,38},{7,39},{8,40},{9,... | collective-permute-start | bytes 3080 | tf_op jit(solution)/shard_map/ppermute | solution.py:10
  202.4 14.6 %collective-permute-start.13 = (bf16[2,2,128]{2,0,1:T(2,128)(2,1)S(1)}, bf16[2,2,128]{2,0,1:T(2,128)(2,1)S(1)}, u32[]{:S(2)}, u32[]{:S(2)}) collective-permute-start(bf16[2,2,128]{2,0,1:T(2,128)(2,1)S(1)} %select_convert_fusion.6), channel_id=1, source_target_pairs={{0,32},{1,33},{2,34},{3,35},{4,36},{5,37},{6,38},{7,39},{8,40},{9,... | collective-permute-start | bytes 3080 | tf_op jit(solution)/shard_map/ppermute | solution.py:10
  217.0 15.2 %collective-permute-start.19 = (bf16[1,2,128]{2,0,1:T(2,128)(2,1)S(1)}, bf16[1,2,128]{2,0,1:T(2,128)(2,1)S(1)}, u32[]{:S(2)}, u32[]{:S(2)}) collective-permute-start(bf16[1,2,128]{2,0,1:T(2,128)(2,1)S(1)} %fusion.60), channel_id=1, source_target_pairs={{0,16},{1,17},{2,18},{3,19},{4,20},{5,21},{6,22},{7,23},{8,24},{9,... | collective-permute-start | bytes 1544 | tf_op jit(solution)/shard_map/ppermute | solution.py:10
  221.4 19.0 %copy-start.1 = (bf16[2,1,128,384]{3,2,1,0:T(8,128)(2,1)S(1)}, bf16[2,1,128,384]{3,2,1,0:T(8,128)(2,1)}, u32[]{:S(2)}) copy-start(bf16[2,1,128,384]{3,2,1,0:T(8,128)(2,1)} %param.6) | copy-start | bytes 589828
  221.5 7.9 %collective-permute-start.14 = (bf16[2,2,128,384]{2,3,0,1:T(8,128)(2,1)S(1)}, bf16[2,2,128,384]{2,3,0,1:T(8,128)(2,1)S(1)}, u32[]{:S(2)}, u32[]{:S(2)}) collective-permute-start(bf16[2,2,128,384]{2,3,0,1:T(8,128)(2,1)S(1)} %select_convert_fusion.1), channel_id=1, source_target_pairs={{0,32},{1,33},{2,34},{3,35},{4,36},{5,37},{6,38},{7,39},{8,40},{9,... | collective-permute-start | bytes 1179656 | tf_op jit(solution)/shard_map/ppermute | solution.py:10
  222.2 10.0 %collective-permute-start.15 = (bf16[1,2,128]{2,0,1:T(2,128)(2,1)S(1)}, bf16[1,2,128]{2,0,1:T(2,128)(2,1)S(1)}, u32[]{:S(2)}, u32[]{:S(2)}) collective-permute-start(bf16[1,2,128]{2,0,1:T(2,128)(2,1)S(1)} %fusion.57), channel_id=1, source_target_pairs={{0,16},{1,17},{2,18},{3,19},{4,20},{5,21},{6,22},{7,23},{8,24},{9,... | collective-permute-start | bytes 1544 | tf_op jit(solution)/shard_map/ppermute | solution.py:10
  229.6 10.9 %collective-permute-start.16 = (bf16[1,2,128,384]{2,3,0,1:T(8,128)(2,1)S(1)}, bf16[1,2,128,384]{2,3,0,1:T(8,128)(2,1)S(1)}, u32[]{:S(2)}, u32[]{:S(2)}) collective-permute-start(bf16[1,2,128,384]{2,3,0,1:T(8,128)(2,1)S(1)} %select_convert_fusion.2), channel_id=1, source_target_pairs={{0,16},{1,17},{2,18},{3,19},{4,20},{5,21},{6,22},{7,23},{8,24},{9,... | collective-permute-start | bytes 589832 | tf_op jit(solution)/shard_map/ppermute | solution.py:10
  240.4 29.6 %slice-start = ((s8[7962624]{0:T(1024)(128)(4,1)}), s8[4194304]{0:T(1024)(128)(4,1)S(1)}, s32[]{:S(2)}) async-start(s8[7962624]{0:T(1024)(128)(4,1)} %bitcast.108), calls=%async_computation | async-start | bytes 8388608
  241.1 2.5 collective-permute-start.20
  243.6 16.2 %collective-permute-start.22 = (bf16[4,1,128,384]{3,2,0,1:T(8,128)(2,1)S(1)}, bf16[4,1,128,384]{3,2,0,1:T(8,128)(2,1)S(1)}, u32[]{:S(2)}, u32[]{:S(2)}) collective-permute-start(bf16[4,1,128,384]{3,2,0,1:T(8,128)(2,1)S(1)} %pad_maximum_fusion.4), channel_id=1, source_target_pairs={{1,0},{2,1},{3,2},{4,3},{5,4},{6,5},{7,6},{8,7},{9,8},{10,9},{11,1... | collective-permute-start | bytes 1179656 | tf_op jit(solution)/shard_map/ppermute | solution.py:37
  251.0 17.2 %collective-permute-start.21 = (bf16[4,1,128,384]{3,2,0,1:T(8,128)(2,1)S(1)}, bf16[4,1,128,384]{3,2,0,1:T(8,128)(2,1)S(1)}, u32[]{:S(2)}, u32[]{:S(2)}) collective-permute-start(bf16[4,1,128,384]{3,2,0,1:T(8,128)(2,1)S(1)} %pad_maximum_fusion.4), channel_id=1, source_target_pairs={{0,1},{1,2},{2,3},{3,4},{4,5},{5,6},{6,7},{7,8},{8,9},{9,10},{10,1... | collective-permute-start | bytes 1179656 | tf_op jit(solution)/shard_map/ppermute | solution.py:35
  268.8 2.1 slice-start.1
where the time goes:
time: 275 us; the launch traced here: 274 us
  waiting for transfers between devices  165 us (60%)
  starting transfers between devices  61.6 us (22%)
  matrix products  22.6 us (8%)
  other arithmetic  18.4 us (7%)
  local copies, waits for them, and re-layouts  6.49 us (2%)
    ppermute x20, waiting for transfers between devices, partner_2(): lax.ppermute(shard, axis, [(i, i ^ 1 << stride) for i in range(lax.axis_s...  149 us
    ppermute x20, starting transfers between devices, partner_2(): lax.ppermute(shard, axis, [(i, i ^ 1 << stride) for i in range(lax.axis_s...  50.9 us
    reduce_sum x1, other arithmetic, per_device(): total = jnp.sum(expo, axis=-1)  8.68 us
    ppermute x1, waiting for transfers between devices, padded_2(): lax.ppermute(tail, axis, [(i, (i + 1) % count) for i in range(ends)])  8.34 us
    dot_general x1, matrix products, per_device(): jnp.einsum('mfqd,fkd->mfqk', query_stack, key_rows, preferred_element_typ...  8.15 us
    dot_general x1, matrix products, per_device(): jnp.einsum('mfqk,fkd->mfqd', probs, value_rows, preferred_element_type=jn...  7.72 us
    ppermute x1, starting transfers between devices, padded_2(): lax.ppermute(head, axis, [((i + 1) % count, i) for i in range(ends)])  7.35 us
    ppermute x1, waiting for transfers between devices, padded_2(): lax.ppermute(head, axis, [((i + 1) % count, i) for i in range(ends)])  6.96 us
  transfers between devices with their start and end apart: 23, of which 16 were waited for; matrix products, arithmetic and copies ran while one was open for 10% of the time, Pallas kernels for 0%

commit v1 on v0

v1 whole, which is shorter than its diff:
```python
import math

import jax
import jax.numpy as jnp
from jax import lax
from jax.sharding import Mesh
from jax.sharding import PartitionSpec as P

ROW_AXES = ("x", "z", "y")


def rms_rows(values):
    return values * lax.rsqrt(jnp.mean(values * values, axis=-1, keepdims=True) + 1e-06)


def project(flat_rows, weight):
    return jnp.dot(flat_rows, weight, preferred_element_type=jnp.float32).astype(jnp.bfloat16)


def row_shift(block, forward):
    count = 1
    for name in ROW_AXES:
        count *= lax.axis_size(name)
    if forward:
        route = [(i, i + 1) for i in range(count - 1)]
    else:
        route = [(i + 1, i) for i in range(count - 1)]
    return lax.ppermute(block, ROW_AXES, route)


def per_device(features, query_weight, key_weight, value_weight, out_weight, conv_weight):
    frames, rows, cols, width = features.shape
    count = rows * cols
    widened = features.astype(jnp.float32)
    normed = rms_rows(widened).astype(jnp.bfloat16)
    flat = normed.reshape(frames * count, width)
    scale = 1.0 / math.sqrt(width)

    query = project(flat, query_weight).reshape(frames, count, width)
    query_all = lax.all_gather(query, "z", axis=1, tiled=True)
    normed_all = lax.all_gather(normed.reshape(frames, count, width), ("x", "y"), axis=1, tiled=True)
    keys_in = normed_all.reshape(-1, width)
    key_rows = project(keys_in, key_weight).reshape(frames, -1, width)
    value_rows = project(keys_in, value_weight).reshape(frames, -1, width)

    scores = jnp.einsum("fqd,fkd->fqk", query_all, key_rows, preferred_element_type=jnp.float32) * scale
    highest = lax.pmax(jnp.max(scores, axis=-1), "z")
    expo = jnp.exp(scores - highest[..., None])
    total = jnp.sum(expo, axis=-1)
    probs = expo.astype(jnp.bfloat16)
    summed = jnp.einsum("fqk,fkd->fqd", probs, value_rows, preferred_element_type=jnp.float32)
    summed = lax.psum_scatter(summed.astype(jnp.bfloat16), "z", scatter_dimension=1, tiled=True)
    total = lax.psum_scatter(total, "z", scatter_dimension=1, tiled=True)
    attended = (summed.astype(jnp.float32) / total[:, :, None]).astype(jnp.bfloat16)

    projected = jnp.dot(attended.reshape(-1, width), out_weight, preferred_element_type=jnp.float32)
    mixed = (widened + projected.reshape(features.shape)).astype(jnp.bfloat16)
    mixed_wide = mixed.astype(jnp.float32)
    activated = jax.nn.silu(rms_rows(mixed_wide)).astype(jnp.bfloat16)

    earlier = lax.ppermute(activated, "tm", [(0, 1)])
    stacked = jnp.concatenate([earlier, activated], axis=0)
    above = row_shift(stacked, True)
    below = row_shift(stacked, False)
    padded = jnp.concatenate([above, stacked, below], axis=1)
    padded = jnp.pad(padded, ((0, 0), (0, 0), (1, 1), (0, 0)))
    patches = []
    for tap_time in range(3):
        for tap_row in range(3):
            for tap_col in range(3):
                patches.append(
                    padded[
                        tap_time : tap_time + frames,
                        tap_row : tap_row + rows,
                        tap_col : tap_col + cols,
                    ]
                )
    columns = jnp.concatenate(patches, axis=-1).reshape(frames * count, 27 * width)
    conv = jnp.dot(
        columns, conv_weight.reshape(27 * width, width), preferred_element_type=jnp.float32
    )
    return (mixed_wide + conv.reshape(features.shape)).astype(jnp.bfloat16)


def solution(mesh):
    sizes = dict(zip(mesh.axis_names, mesh.devices.shape))
    tile = sizes["tile"]
    y = 4
    z = 8
    x = tile // (y * z)
    fine = Mesh(mesh.devices.reshape(sizes["tm"], x, z, y), ("tm", *ROW_AXES))
    spec = P("tm", ROW_AXES, None, None)
    in_specs = (spec, P(), P(), P(), P(), P())
    return jax.shard_map(
        per_device, mesh=fine, in_specs=in_specs, out_specs=spec, check_vma=False
    )
```

time: 275 us -> 260 us (0.945)
  starting transfers between devices: 61.6 us -> 9.04 us
  blocking collectives: 0 us -> 16.1 us
  matrix products: 22.6 us -> 36.3 us
  between operations: 0.45 us -> 13.4 us
  other arithmetic: 18.4 us -> 11.4 us
  waiting for transfers between devices: 165 us -> 169 us
    ppermute x23 -> x3, waiting for transfers between devices: 165 us -> 16.3 us  [the longest x2 15.3 us: row_shift(): return lax.ppermute(block, ROW_AXES, route)]
    all_gather x0 -> x2, waiting for transfers between devices: none -> 86.4 us  [the longest x1 53.1 us: per_device(): lax.all_gather(normed.reshape(frames, count, width), ('x', 'y'), axis=1,...]
    ppermute x23 -> x3, starting transfers between devices: 61.6 us -> 8.73 us  [the longest x2 7.43 us: row_shift(): return lax.ppermute(block, ROW_AXES, route)]
    reduce_scatter x0 -> x1, waiting for transfers between devices: none -> 40.8 us  [per_device(): lax.psum_scatter(summed.astype(jnp.bfloat16), 'z', scatter_dimension=1, t...]
    unnamed x0 -> x5, waiting for transfers between devices: none -> 25.5 us
    pmax x0 -> x1, blocking collectives: none -> 16.1 us  [per_device(): highest = lax.pmax(jnp.max(scores, axis=-1), 'z')]
    dot_general x3, matrix products: 2.72 us -> 9.83 us  [project(): jnp.dot(flat_rows, weight, preferred_element_type=jnp.float32)]
    dot_general x2, matrix products: 15.9 us -> 21.1 us  [the longest x1 11.5 us: per_device(): jnp.einsum('fqk,fkd->fqd', probs, value_rows, preferred_element_type=jnp....]
  transfers between devices with their start and end apart: 23 -> 7, of which waited for: 16 -> 7; matrix products, arithmetic and copies ran while one was open for 10% -> 9% of each run, Pallas kernels for 0% -> 0%
where the time goes in v1:
time: 260 us; the launch traced here: 259 us
  waiting for transfers between devices  169 us (65%)
  matrix products  36.3 us (14%)
  blocking collectives  16.1 us (6%)
  between operations  13.4 us (5%)
  other arithmetic  11.4 us (4%)
  starting transfers between devices  9.04 us (3%)
  local copies, waits for them, and re-layouts  3.88 us (1%)
    all_gather x1, waiting for transfers between devices, per_device(): lax.all_gather(normed.reshape(frames, count, width), ('x', 'y'), axis=1,...  53.1 us
    reduce_scatter x1, waiting for transfers between devices, per_device(): lax.psum_scatter(summed.astype(jnp.bfloat16), 'z', scatter_dimension=1, t...  40.8 us
    all_gather x1, waiting for transfers between devices, per_device(): query_all = lax.all_gather(query, 'z', axis=1, tiled=True)  33.3 us
    unnamed x5, waiting for transfers between devices  25.5 us
    pmax x1, blocking collectives, per_device(): highest = lax.pmax(jnp.max(scores, axis=-1), 'z')  16.1 us
    ppermute x2, waiting for transfers between devices, row_shift(): return lax.ppermute(block, ROW_AXES, route)  15.3 us
    dot_general x1, matrix products, per_device(): jnp.einsum('fqk,fkd->fqd', probs, value_rows, preferred_element_type=jnp....  11.5 us
    dot_general x3, matrix products, project(): jnp.dot(flat_rows, weight, preferred_element_type=jnp.float32)  9.83 us
  transfers between devices with their start and end apart: 7, of which 7 were waited for; matrix products, arithmetic and copies ran while one was open for 9% of the time, Pallas kernels for 0%

profile of v1, /device:TPU:2, one launch (start us, length us, event | category | flops | bytes accessed | tf_op | source)
XLA Modules:
  0.0 259.0 jit_solution(6664018388497770649)
XLA Ops:
  6.5 0.0 copy-start
  6.5 0.0 all-gather.6.cloned.1.call-start
  6.5 1.1 fusion.30
  7.6 1.7 fusion.31
  9.3 0.0 all-gather.6.cloned.1.call-update
  9.4 0.0 all-gather.4.cloned.1.call-start
  9.4 2.0 convolution_convert_fusion.2
  11.4 0.0 all-gather.4.cloned.1.call-update
  11.5 0.0 reduce-scatter.7.cloned.1.call-start
  11.5 53.1 %all-gather.6.cloned.1.call-done = bf16[2,1,2048,384]{3,2,0,1:T(8,128)(2,1)} async-done(((bf16[2,1,128,384]{3,2,0,1:T(8,128)(2,1)}), bf16[2,1,2048,384]{3,2,0,1:T(8,128)(2,1)}) %all-gather.6.cloned.1.call-update) | async-done | bytes 3145744 | tf_op jit(solution)/shard_map/all_gather | solution.py:41
  64.6 0.0 copy-start.1
  64.6 0.0 copy-start.3
  64.6 0.0 copy-done
  64.6 5.7 %convolution_convert_fusion = bf16[4096,384]{1,0:T(8,128)(2,1)} fusion(bf16[4096,384]{1,0:T(8,128)(2,1)} %bitcast.58, bf16[384,384]{1,0:T(8,128)(2,1)S(1)} %copy-done), kind=kOutput, calls=%fused_computation.7 | convolution fusion | flops 1209532416 | bytes 6586368 | tf_op jit(solution)/shard_map/dot_general | solution.py:17
  70.3 0.0 copy-done.1
  70.3 0.0 copy-done.3
  70.3 2.1 convolution_convert_fusion.1
  72.4 33.3 %all-gather.4.cloned.1.call-done = bf16[2,1024,384]{2,1,0:T(8,128)(2,1)} async-done(((bf16[2,128,384]{2,1,0:T(8,128)(2,1)}), bf16[2,1024,384]{2,1,0:T(8,128)(2,1)}) %all-gather.4.cloned.1.call-update) | async-done | bytes 1572880 | tf_op jit(solution)/shard_map/all_gather | solution.py:40
  105.7 9.6 %multiply_reduce_fusion = (f32[2,1024]{1,0:T(2,128)S(1)}, f32[2,1024,2048]{2,1,0:T(8,128)}) fusion(bf16[2,1024,384]{2,1,0:T(8,128)(2,1)} %all-gather.4.cloned.1.call-done, bf16[2,2048,384]{2,1,0:T(8,128)(2,1)S(1)} %bitcast.60), kind=kOutput, calls=%fused_computation.1 | convolution fusion | flops 3229612032 | bytes 21504000 | tf_op jit(solution)/shard_map/fqd,fkd->fqk/dot_general | solution.py:46
  115.3 16.1 %pmax.7 = f32[2,1024]{1,0:T(2,128)S(1)} all-reduce(f32[2,1024]{1,0:T(2,128)S(1)} %get-tuple-element.5), channel_id=1, replica_groups=mesh['tm'=2,'x'=4,'z'=8,'y'=4] {'z'}, use_global_device_ids=true, to_apply=%region_2.0 | all-reduce | flops 2048 | bytes 16384 | tf_op jit(solution)/shard_map/pmax | solution.py:47
  131.4 0.0 copy-start.2
  131.4 7.7 %fusion = f32[2,1024]{1,0:T(2,128)S(1)} fusion(f32[2,1024,2048]{2,1,0:T(8,128)} %get-tuple-element.6, f32[2,1024]{1,0:T(2,128)S(1)} %pmax.7), kind=kLoop, calls=%fused_computation.2 | loop fusion | flops 12580864 | bytes 16793600 | tf_op jit(solution)/shard_map/reduce_sum | solution.py:49
  139.2 1.0 copy.11
  140.2 0.0 reduce-scatter.7.cloned.1.call-update
  140.2 0.2 reduce-scatter.5.cloned.1.call-start
  140.4 0.0 copy-done.2
  140.5 11.5 %fusion.9 = bf16[2,1024,384]{2,1,0:T(8,128)(2,1)} fusion(bf16[2,2048,384]{2,1,0:T(8,128)(2,1)S(1)} %bitcast.61, f32[2,1024,2048]{2,1,0:T(8,128)} %get-tuple-element.6, f32[2,1024]{1,0:T(2,128)S(1)} %pmax.7), kind=kOutput, calls=%fused_computation.14 | convolution fusion | flops 3234594816 | bytes 21504000 | tf_op jit(solution)/shard_map/fqk,fkd->fqd/dot_general | solution.py:51
  152.0 0.0 reduce-scatter.5.cloned.1.call-update
  152.0 25.5 %reduce-scatter.7.cloned.1.call-done = f32[128,2]{1,0:T(8,128)} async-done(((f32[1024,2]{1,0:T(8,128)}), f32[128,2]{1,0:T(8,128)}) %reduce-scatter.7.cloned.1.call-update) | async-done | bytes 1040
  177.5 0.9 copy.12
  178.4 40.8 %reduce-scatter.5.cloned.1.call-done = bf16[2,128,384]{2,1,0:T(8,128)(2,1)} async-done(((bf16[2,1024,384]{2,1,0:T(8,128)(2,1)}), bf16[2,128,384]{2,1,0:T(8,128)(2,1)}) %reduce-scatter.5.cloned.1.call-update) | async-done | bytes 196624 | tf_op jit(solution)/shard_map/reduce_scatter | solution.py:52
  219.1 0.0 slice-start
  219.1 1.7 multiply_reduce_fusion.1
  220.9 0.2 multiply_convert_fusion
  221.1 1.3 collective-permute-start
  222.4 1.0 collective-permute-done
  223.5 5.5 %collective-permute-start.2 = (bf16[4,1,128,384]{3,2,0,1:T(8,128)(2,1)S(1)}, bf16[4,1,128,384]{3,2,0,1:T(8,128)(2,1)S(1)}, u32[]{:S(2)}, u32[]{:S(2)}) collective-permute-start(bf16[4,1,128,384]{3,2,0,1:T(8,128)(2,1)S(1)} %pad_maximum_fusion), channel_id=1, source_target_pairs={{1,0},{2,1},{3,2},{4,3},{5,4},{6,5},{7,6},{8,7},{9,8},{10,9},{11,1... | collective-permute-start | bytes 1179656 | tf_op jit(solution)/shard_map/ppermute | solution.py:28
  229.0 1.9 collective-permute-start.1
  230.9 7.0 %collective-permute-done.2 = bf16[4,1,128,384]{3,2,0,1:T(8,128)(2,1)S(1)} collective-permute-done((bf16[4,1,128,384]{3,2,0,1:T(8,128)(2,1)S(1)}, bf16[4,1,128,384]{3,2,0,1:T(8,128)(2,1)S(1)}, u32[]{:S(2)}, u32[]{:S(2)}) %collective-permute-start.2) | collective-permute-done | bytes 393248 | tf_op jit(solution)/shard_map/ppermute | solution.py:28
  237.9 8.3 %collective-permute-done.1 = bf16[4,1,128,384]{3,2,0,1:T(8,128)(2,1)S(1)} collective-permute-done((bf16[4,1,128,384]{3,2,0,1:T(8,128)(2,1)S(1)}, bf16[4,1,128,384]{3,2,0,1:T(8,128)(2,1)S(1)}, u32[]{:S(2)}, u32[]{:S(2)}) %collective-permute-start.1) | collective-permute-done | bytes 393248 | tf_op jit(solution)/shard_map/ppermute | solution.py:28
  246.2 0.3 select_maximum_fusion
  246.6 0.1 slice_dynamic-update-slice_fusion.21
  246.8 0.1 slice_dynamic-update-slice_fusion.19
  246.8 0.0 slice-start.1
  246.9 0.1 slice_dynamic-update-slice_fusion.16
  247.1 0.1 slice_dynamic-update-slice_fusion.13
  247.2 0.1 slice_dynamic-update-slice_fusion.11
  247.4 0.1 slice_dynamic-update-slice_fusion.8
  247.5 0.1 slice_dynamic-update-slice_fusion.5
  247.6 0.2 constant_dynamic-update-slice_fusion
  247.8 0.1 slice_dynamic-update-slice_fusion.3
  248.0 0.1 slice_dynamic-update-slice_fusion
  248.1 0.0 slice-done
  248.1 0.8 slice-done.1
  248.9 3.6 %fusion.27 = bf16[2,1,128,384]{3,2,1,0:T(8,128)(2,1)} fusion(f32[2,1,128,384]{3,2,0,1:T(8,128)S(1)} %get-tuple-element.8, bf16[10368,384,1]{1,0,2:T(8,128)(2,1)S(1)} %bitcast.68, bf16[2,1,128,10368]{3,2,0,1:T(8,128)(2,1)S(1)} %slice_dynamic-update-slice_fusion), kind=kOutput, calls=%fused_computation.28 | convolution fusion | flops 2038628352 | bytes 13860864 | tf_op jit(solution)/shard_map/dot_general | solution.py:79
  (21 shorter events, 0.6 us)
Async XLA Ops:
  6.5 58.0 %copy-start = (bf16[384,384]{1,0:T(8,128)(2,1)S(1)}, bf16[384,384]{1,0:T(8,128)(2,1)}, u32[]{:S(2)}) copy-start(bf16[384,384]{1,0:T(8,128)(2,1)} %param.9) | copy-start | bytes 884740
  6.5 58.0 %all-gather.6.cloned.1.call-start = ((), (), s32[]{:S(2)}) async-start(), calls=%async_computation.4 | async-start | bytes 3342336 | tf_op jit(solution)/shard_map/all_gather | solution.py:41
  9.4 96.4 %all-gather.4.cloned.1.call-start = ((), (), s32[]{:S(2)}) async-start(), calls=%async_computation.2 | async-start | bytes 1769472 | tf_op jit(solution)/shard_map/all_gather | solution.py:40
  11.5 166.0 %reduce-scatter.7.cloned.1.call-start = ((), (), s32[]{:S(2)}) async-start(), calls=%async_computation.5 | async-start | bytes 589824
  64.6 5.7 %copy-start.1 = (bf16[2,1,2048,384]{3,2,0,1:T(8,128)(2,1)S(1)}, bf16[2,1,2048,384]{3,2,0,1:T(8,128)(2,1)}, u32[]{:S(2)}) copy-start(bf16[2,1,2048,384]{3,2,0,1:T(8,128)(2,1)} %all-gather.6.cloned.1.call-done) | copy-start | bytes 9437188
  64.6 5.8 %copy-start.3 = (bf16[384,384]{1,0:T(8,128)(2,1)S(1)}, bf16[384,384]{1,0:T(8,128)(2,1)}, u32[]{:S(2)}) copy-start(bf16[384,384]{1,0:T(8,128)(2,1)} %param.8) | copy-start | bytes 884740
  131.4 9.0 %copy-start.2 = (bf16[4096,384]{1,0:T(8,128)(2,1)S(1)}, bf16[4096,384]{1,0:T(8,128)(2,1)}, u32[]{:S(2)}) copy-start(bf16[4096,384]{1,0:T(8,128)(2,1)} %convolution_convert_fusion) | copy-start | bytes 9437188
  140.2 78.9 %reduce-scatter.5.cloned.1.call-start = ((), (), s32[]{:S(2)}) async-start(), calls=%async_computation.3 | async-start | bytes 1769472 | tf_op jit(solution)/shard_map/reduce_scatter | solution.py:52
  219.1 28.9 %slice-start = ((s8[7962624]{0:T(1024)(128)(4,1)}), s8[4194304]{0:T(1024)(128)(4,1)S(1)}, s32[]{:S(2)}) async-start(s8[7962624]{0:T(1024)(128)(4,1)} %bitcast.66), calls=%async_computation.6 | async-start | bytes 8388608
  221.1 2.4 collective-permute-start
  223.5 14.4 %collective-permute-start.2 = (bf16[4,1,128,384]{3,2,0,1:T(8,128)(2,1)S(1)}, bf16[4,1,128,384]{3,2,0,1:T(8,128)(2,1)S(1)}, u32[]{:S(2)}, u32[]{:S(2)}) collective-permute-start(bf16[4,1,128,384]{3,2,0,1:T(8,128)(2,1)S(1)} %pad_maximum_fusion), channel_id=1, source_target_pairs={{1,0},{2,1},{3,2},{4,3},{5,4},{6,5},{7,6},{8,7},{9,8},{10,9},{11,1... | collective-permute-start | bytes 1179656 | tf_op jit(solution)/shard_map/ppermute | solution.py:28
  229.0 17.2 %collective-permute-start.1 = (bf16[4,1,128,384]{3,2,0,1:T(8,128)(2,1)S(1)}, bf16[4,1,128,384]{3,2,0,1:T(8,128)(2,1)S(1)}, u32[]{:S(2)}, u32[]{:S(2)}) collective-permute-start(bf16[4,1,128,384]{3,2,0,1:T(8,128)(2,1)S(1)} %pad_maximum_fusion), channel_id=1, source_target_pairs={{0,1},{1,2},{2,3},{3,4},{4,5},{5,6},{6,7},{7,8},{8,9},{9,10},{10,1... | collective-permute-start | bytes 1179656 | tf_op jit(solution)/shard_map/ppermute | solution.py:28
  246.8 2.1 slice-start.1
Sparse Core Ops, SparseCore 0:
  9.8 54.7 all-gather.5
  66.4 39.3 all-gather.3
  140.3 37.1 reduce-scatter.6
  179.9 39.1 reduce-scatter.4
